TPU v7x, 128 devices: a whole 4x4x4 slice. The times are simulated.
128 devices in a mesh: req: 4 (over z), seq: 32 (over x, y, core).
Axes of the slice: x: 4, y: 4, z: 4, core: 2. Of those that a mesh axis runs over, the one named last changes fastest.
Arguments:
- short_tokens: bfloat16 [256, 4, 1024], P(('req', 'seq')), may hold values from -6 to 6
- long_tokens: bfloat16 [8, 4, 1024], P('req'), may hold values from -6 to 6
- short_keys: bfloat16 [256, 1024, 1024], P(('req', 'seq'))
- short_values: bfloat16 [256, 1024, 1024], P(('req', 'seq')), may hold values from -6 to 6
- long_keys: bfloat16 [8, 8192, 1024], P('req', 'seq')
- long_values: bfloat16 [8, 8192, 1024], P('req', 'seq'), may hold values from -6 to 6
- short_lengths: int32 [256], P(('req', 'seq')), may hold values from 512 to 1024
- long_lengths: int32 [8], P('req'), may hold values from 4096 to 8192
- attn_gain: float32 [1024], replicated, may hold values from 0.5 to 1.5
- ffn_gain: float32 [1024], replicated, may hold values from 0.5 to 1.5
- w_query: bfloat16 [1024, 1024], P(None, 'req'), may hold values from -0.1875 to 0.1875
- w_key: bfloat16 [1024, 1024], P(None, 'req'), may hold values from -0.1875 to 0.1875
- w_value: bfloat16 [1024, 1024], P(None, 'req'), may hold values from -0.1875 to 0.1875
- w_out: bfloat16 [1024, 1024], P('req'), may hold values from -0.1875 to 0.1875
- w_up: bfloat16 [1024, 4096], P(None, 'req'), may hold values from -0.1875 to 0.1875
- w_down: bfloat16 [4096, 1024], P('req'), may hold values from -0.09375 to 0.09375
Outputs:
- short_hidden: bfloat16 [256, 4, 1024], P(('req', 'seq'))
- long_hidden: bfloat16 [8, 4, 1024], P('req')
- short_new_keys: bfloat16 [256, 4, 1024], P(('req', 'seq'))
- short_new_values: bfloat16 [256, 4, 1024], P(('req', 'seq'))
- long_new_keys: bfloat16 [8, 4, 1024], P('req')
- long_new_values: bfloat16 [8, 4, 1024], P('req')
All inputs are finite; a program needn't handle non-finite values.
Results may differ from a plain program's by a relative error of at most 0.011.
Values may be sent and summed in bfloat16 or wider, within the bound.
No kernel may reach another device: no remote copies, remote signals or barrier semaphores. Data moves between devices by JAX's collectives and lax.ppermute only.
A program may use at most 128 MiB of HBM per device.

v0:
```python
import jax
import jax.numpy as jnp
from jax import lax
from jax.sharding import PartitionSpec as P

H = 16
HD = 64
masked_score = -1e30


def layer_norm(rows, gain):
    mean = jnp.mean(rows, axis=-1, keepdims=True)
    centred = rows - mean
    spread = jnp.mean(centred * centred, axis=-1, keepdims=True)
    return centred * lax.rsqrt(spread + 1e-05) * gain


def partial_block(query, keys, values, valid):
    scores = jnp.einsum("rthd,rphd->rhtp", query, keys, preferred_element_type=jnp.float32) * 0.125
    scores = jnp.where(valid, scores, masked_score)
    peak = jnp.max(scores, axis=-1)
    weights = jnp.where(valid, jnp.exp(scores - peak[..., None]), 0.0)
    total = jnp.sum(weights, axis=-1)
    output = jnp.einsum(
        "rhtp,rphd->rhtd", weights.astype(jnp.bfloat16), values, preferred_element_type=jnp.float32
    )
    return (peak, total, output)


def join(first, second):
    peak = jnp.maximum(first[0], second[0])
    scale_one = jnp.exp(first[0] - peak)
    scale_two = jnp.exp(second[0] - peak)
    total = first[1] * scale_one + second[1] * scale_two
    output = first[2] * scale_one[..., None] + second[2] * scale_two[..., None]
    return (peak, total, output)


def merge_long(partial_value):
    peak, total, output = partial_value
    top = lax.pmax(peak, "seq")
    scale = jnp.exp(peak - top)
    total_sum, output_sum = lax.psum((total * scale, output * scale[..., None]), "seq")
    return (top, total_sum, output_sum)


def shards(
    short_tokens,
    long_tokens,
    short_keys,
    short_values,
    long_keys,
    long_values,
    short_lengths,
    long_lengths,
    attn_gain,
    ffn_gain,
    w_query,
    w_key,
    w_value,
    w_out,
    w_up,
    w_down,
):
    short_count = short_tokens.shape[0]
    long_count = long_tokens.shape[0]
    steps = short_tokens.shape[1]
    width = short_tokens.shape[2]
    req_count = short_count + long_count
    rows_count = req_count * steps
    groups = lax.axis_size("req")
    block = long_keys.shape[1]
    anchor = lax.axis_index("seq") * block
    cache_short_k = short_keys.reshape(short_count, short_keys.shape[1], H, HD)
    cache_short_v = short_values.reshape(short_count, short_keys.shape[1], H, HD)
    cache_long_k = long_keys.reshape(long_count, block, H, HD)
    cache_long_v = long_values.reshape(long_count, block, H, HD)
    short_valid = (jnp.arange(short_keys.shape[1])[None, :] < short_lengths[:, None])[
        :, None, None, :
    ]
    long_valid = ((anchor + jnp.arange(block))[None, :] < long_lengths[:, None])[:, None, None, :]
    stacked = jnp.concatenate([w_query, w_key, w_value], 1)
    local = w_query.shape[1]
    fresh_ids = jnp.arange(steps)
    fresh_valid = (fresh_ids[None, :] <= fresh_ids[:, None])[None, None, :, :]
    rows = (
        jnp.concatenate([short_tokens, long_tokens], 0)
        .reshape(rows_count, width)
        .astype(jnp.float32)
    )
    normed = layer_norm(rows, attn_gain).astype(jnp.bfloat16)
    project_spread = jnp.dot(
        lax.all_gather(normed, "req", axis=0, tiled=True),
        stacked,
        preferred_element_type=jnp.float32,
    ).astype(jnp.bfloat16)
    moved = lax.all_to_all(project_spread, "req", split_axis=0, concat_axis=1, tiled=True)
    moved = moved.reshape(rows_count, groups, 3, local)
    query = moved[:, :, 0].reshape(req_count, steps, H, HD)
    key_now = moved[:, :, 1].reshape(req_count, steps, width)
    value_now = moved[:, :, 2].reshape(req_count, steps, width)
    fresh_k = key_now.reshape(req_count, steps, H, HD)
    fresh_v = value_now.reshape(req_count, steps, H, HD)
    fresh = partial_block(query, fresh_k, fresh_v, fresh_valid)
    short_part = partial_block(query[:short_count], cache_short_k, cache_short_v, short_valid)
    long_part = merge_long(
        partial_block(query[short_count:], cache_long_k, cache_long_v, long_valid)
    )
    cache_part = jax.tree.map(
        lambda first, second: jnp.concatenate([first, second], 0), short_part, long_part
    )
    peak, total, output = join(cache_part, fresh)
    attended = output / total[..., None]
    attended = attended.transpose(0, 2, 1, 3).reshape(rows_count, width).astype(jnp.bfloat16)
    spread = lax.all_to_all(attended, "req", split_axis=1, concat_axis=0, tiled=True)
    mixed = rows + lax.psum_scatter(
        jnp.dot(spread, w_out, preferred_element_type=jnp.float32),
        "req",
        scatter_dimension=0,
        tiled=True,
    )
    normed_ffn = layer_norm(mixed, ffn_gain).astype(jnp.bfloat16)
    hidden = jax.nn.gelu(
        jnp.dot(
            lax.all_gather(normed_ffn, "req", axis=0, tiled=True),
            w_up,
            preferred_element_type=jnp.float32,
        ),
        approximate=False,
    ).astype(jnp.bfloat16)
    result = mixed + lax.psum_scatter(
        jnp.dot(hidden, w_down, preferred_element_type=jnp.float32),
        "req",
        scatter_dimension=0,
        tiled=True,
    )
    states = result.astype(jnp.bfloat16).reshape(req_count, steps, width)
    return (
        states[:short_count],
        states[short_count:],
        key_now[:short_count],
        value_now[:short_count],
        key_now[short_count:],
        value_now[short_count:],
    )


def solution(mesh):
    in_specs = (
        P(("req", "seq"), None, None),
        P("req", None, None),
        P(("req", "seq"), None, None),
        P(("req", "seq"), None, None),
        P("req", "seq", None),
        P("req", "seq", None),
        P(("req", "seq")),
        P("req"),
        P(),
        P(),
        P(None, "req"),
        P(None, "req"),
        P(None, "req"),
        P("req", None),
        P(None, "req"),
        P("req", None),
    )
    out_specs = (
        P(("req", "seq"), None, None),
        P("req", None, None),
        P(("req", "seq"), None, None),
        P(("req", "seq"), None, None),
        P("req", None, None),
        P("req", None, None),
    )
    return jax.shard_map(shards, mesh=mesh, in_specs=in_specs, out_specs=out_specs, check_vma=False)
```

profile of v0, /device:TPU:0, one launch (start us, length us, event | category | flops | bytes accessed | tf_op | source)
XLA Modules:
  0.0 382.5 jit_solution(11535167643442120678)
XLA Ops:
  7.2 0.0 copy-start
  7.2 0.0 copy-start.11
  7.2 1.0 fusion.115
  8.2 0.1 div.23
  8.3 0.9 multiply_reduce_fusion.1
  9.2 0.8 maximum_convert_fusion
  10.0 0.1 rsqrt.20
  10.1 0.8 multiply_convert_fusion.1
  10.8 13.3 %all_gather.6 = bf16[64,1024]{1,0:T(8,128)(2,1)S(1)} all-gather(bf16[16,1024]{1,0:T(8,128)(2,1)S(1)} %multiply_convert_fusion.1), channel_id=1, replica_groups=mesh['req'=4,'seq'=32] {'req'}, dimensions={0}, use_global_device_ids=true | all-gather | bytes 163840 | tf_op jit(solution)/shard_map/all_gather | solution.py:93
  24.2 2.4 fusion.7
  26.5 4.3 %all-to-all-start = ((bf16[4,16,768]{2,1,0:T(8,128)(2,1)}), bf16[4,16,768]{2,1,0:T(8,128)(2,1)S(1)}, u32[]{:S(2)}, u32[]{:S(2)}) async-start(bf16[4,16,768]{2,1,0:T(8,128)(2,1)} %bitcast), calls=%async_computation | async-start | bytes 196608 | tf_op jit(solution)/shard_map/all_to_all | solution.py:97
  30.8 0.1 iota_compare_fusion
  30.9 1.5 copy.151
  32.4 2.3 copy.153
  34.7 6.2 %copy.147 = bf16[2,1024,1024]{1,2,0:T(8,128)(2,1)} copy(bf16[2,1024,1024]{2,1,0:T(8,128)(2,1)} %param.18) | data formatting | bytes 8388608 | tf_op args[2]
  40.9 6.2 %copy.149 = bf16[2,1024,1024]{1,2,0:T(8,128)(2,1)} copy(bf16[2,1024,1024]{2,1,0:T(8,128)(2,1)} %param.19) | data formatting | bytes 8388608 | tf_op args[3]
  47.1 0.0 copy-done.12
  47.1 0.1 broadcast_compare_fusion
  47.2 0.0 all-to-all-done
  47.3 0.8 fusion.120
  48.1 0.1 fusion.121
  48.3 0.1 reshape_reshape_squeeze.6
  48.4 0.7 reshape_squeeze.2
  49.2 1.0 fusion.68
  50.2 0.2 copy.158
  50.4 0.1 fusion.79
  50.5 0.1 fusion.80
  50.6 0.1 copy.171
  50.7 0.8 copy.150
  51.5 0.1 slice.66
  51.6 0.8 copy.146
  52.4 0.1 slice.64
  52.5 0.7 reshape_reshape_squeeze.7
  53.2 0.1 copy.172
  53.3 0.8 copy.162
  54.1 0.3 fusion.123
  54.5 125.1 %pmax.7 = f32[2,16,4]{2,1,0:T(8,128)S(1)} all-reduce(f32[2,16,4]{2,1,0:T(8,128)S(1)} %get-tuple-element.28), channel_id=1, replica_groups=mesh['req'=4,'seq'=32] {'seq'}, use_global_device_ids=true, to_apply=%region_4.5 | all-reduce | flops 128 | bytes 1024 | tf_op jit(solution)/shard_map/pmax | solution.py:41
  179.5 0.2 fusion.64
  179.7 3.1 fusion.124
  182.8 0.4 fusion.15
  183.2 1.2 fusion.17
  184.5 0.4 convolution_multiply_fusion.3
  184.9 123.9 %all-reduce = (f32[2,16,4,64]{3,2,1,0:T(4,128)S(1)}, f32[2,16,4]{2,1,0:T(8,128)S(1)}) all-reduce(f32[2,16,4,64]{3,2,1,0:T(4,128)S(1)} %convolution_multiply_fusion.3, f32[2,16,4]{2,1,0:T(8,128)S(1)} %get-tuple-element.13), channel_id=1, replica_groups=mesh['req'=4,'seq'=32] {'seq'}, use_global_device_ids=true, to_apply=%region_5.6 | all-reduce | flops 8320 | bytes 66560 | tf_op jit(solution)/shard_map/psum | solution.py:43
  308.8 0.3 fusion.14
  309.1 0.1 convert_element_type.54
  309.3 9.8 %all_to_all.32 = bf16[16,4,256]{2,0,1:T(8,128)(2,1)S(1)} all-to-all(bf16[16,4,256]{2,0,1:T(8,128)(2,1)S(1)} %copy.166), channel_id=1, replica_groups=mesh['req'=4,'seq'=32] {'req'}, dimensions={1} | all-to-all | bytes 65536 | tf_op jit(solution)/shard_map/all_to_all | solution.py:115
  319.0 0.9 fusion.127
  319.9 0.0 reduce-scatter.3.cloned.1.call-update
  320.0 0.0 reduce-scatter.5.cloned.1.call-start
  320.0 15.6 %reduce-scatter.3.cloned.1.call-done = f32[16,1024]{1,0:T(8,128)} async-done(((f32[64,1024]{1,0:T(8,128)}), f32[16,1024]{1,0:T(8,128)}) %reduce-scatter.3.cloned.1.call-update) | async-done | bytes 65552 | tf_op jit(solution)/shard_map/reduce_scatter | solution.py:116
  335.6 1.0 fusion.116
  336.6 0.2 multiply_reduce_fusion
  336.8 0.1 multiply_convert_fusion
  336.9 12.0 %all_gather.7 = bf16[64,1024]{1,0:T(8,128)(2,1)S(1)} all-gather(bf16[16,1024]{1,0:T(8,128)(2,1)S(1)} %multiply_convert_fusion), channel_id=1, replica_groups=mesh['req'=4,'seq'=32] {'req'}, dimensions={0}, use_global_device_ids=true | all-gather | bytes 163840 | tf_op jit(solution)/shard_map/all_gather | solution.py:125
  348.9 3.7 fusion.32
  352.6 0.0 reduce-scatter.5.cloned.1.call-update
  352.7 0.6 slice.81
  353.3 0.6 slice.79
  354.0 0.6 slice.77
  354.6 0.6 slice.75
  355.2 18.3 %reduce-scatter.5.cloned.1.call-done = f32[16,1024]{1,0:T(8,128)} async-done(((f32[64,1024]{1,0:T(8,128)}), f32[16,1024]{1,0:T(8,128)}) %reduce-scatter.5.cloned.1.call-update) | async-done | bytes 65552 | tf_op jit(solution)/shard_map/reduce_scatter | solution.py:131
  373.6 0.8 add_convert_fusion
  374.4 0.6 slice.73
  375.0 0.6 slice.71
  (44 shorter events, 0.4 us)
Async XLA Ops:
  7.2 341.7 %copy-start = (bf16[1024,1024]{1,0:T(8,128)(2,1)S(1)}, bf16[1024,1024]{1,0:T(8,128)(2,1)}, u32[]{:S(2)}) copy-start(bf16[1024,1024]{1,0:T(8,128)(2,1)} %param.31) | copy-start | bytes 6291460
  7.2 23.6 %copy-start.11 = (s32[2]{0:T(128)S(1)}, s32[2]{0:T(128)}, u32[]{:S(2)}) copy-start(s32[2]{0:T(128)} %param.22) | copy-start | bytes 28
  26.5 20.7 %all-to-all-start = ((bf16[4,16,768]{2,1,0:T(8,128)(2,1)}), bf16[4,16,768]{2,1,0:T(8,128)(2,1)S(1)}, u32[]{:S(2)}, u32[]{:S(2)}) async-start(bf16[4,16,768]{2,1,0:T(8,128)(2,1)} %bitcast), calls=%async_computation | async-start | bytes 196608 | tf_op jit(solution)/shard_map/all_to_all | solution.py:97
  30.8 304.9 %reduce-scatter.3.cloned.1.call-start = ((), (), s32[]{:S(2)}) async-start(), calls=%async_computation.4 | async-start | bytes 327680 | tf_op jit(solution)/shard_map/reduce_scatter | solution.py:116
  40.9 6.2 %copy-start.12 = (s32[2]{0:T(128)S(1)}, s32[2]{0:T(128)}, u32[]{:S(2)}) copy-start(s32[2]{0:T(128)} %param.23) | copy-start | bytes 28
  179.5 3.7 copy-start.1
  182.8 1.7 copy-start.2
  183.2 125.6 %copy-start.8 = (bf16[4,16,4,4]{3,2,1,0:T(4,128)(2,1)S(1)}, bf16[4,16,4,4]{3,2,1,0:T(4,128)(2,1)}, u32[]{:S(2)}) copy-start(bf16[4,16,4,4]{3,2,1,0:T(4,128)(2,1)} %copy.162) | copy-start | bytes 6148
  183.2 125.6 %copy-start.9 = (bf16[4,4,16,64]{3,2,1,0:T(8,128)(2,1)S(1)}, bf16[4,4,16,64]{3,2,1,0:T(8,128)(2,1)}, u32[]{:S(2)}) copy-start(bf16[4,4,16,64]{3,2,1,0:T(8,128)(2,1)} %reshape_reshape_squeeze.7) | copy-start | bytes 98308
  184.4 134.6 %copy-start.3 = (bf16[256,1024]{1,0:T(8,128)(2,1)S(1)}, bf16[256,1024]{1,0:T(8,128)(2,1)}, u32[]{:S(2)}) copy-start(bf16[256,1024]{1,0:T(8,128)(2,1)} %param.29) | copy-start | bytes 1572868
  184.4 152.4 %copy-start.10 = (f32[1024]{0:T(1024)S(1)}, f32[1024]{0:T(1024)}, u32[]{:S(2)}) copy-start(f32[1024]{0:T(1024)} %param.25) | copy-start | bytes 12292
  320.0 53.6 %reduce-scatter.5.cloned.1.call-start = ((), (), s32[]{:S(2)}) async-start(), calls=%async_computation.5 | async-start | bytes 327680 | tf_op jit(solution)/shard_map/reduce_scatter | solution.py:131
  348.9 3.8 copy-start.7
  348.9 4.4 %copy-start.6 = (bf16[8,4,1,256]{3,2,0,1:T(2,128)(2,1)S(1)}, bf16[8,4,1,256]{3,2,0,1:T(2,128)(2,1)}, u32[]{:S(2)}) copy-start(bf16[8,4,1,256]{3,2,0,1:T(2,128)(2,1)} %get-tuple-element.16) | copy-start | bytes 49156
  348.9 5.0 %copy-start.5 = (bf16[8,4,1,256]{3,2,0,1:T(2,128)(2,1)S(1)}, bf16[8,4,1,256]{3,2,0,1:T(2,128)(2,1)}, u32[]{:S(2)}) copy-start(bf16[8,4,1,256]{3,2,0,1:T(2,128)(2,1)} %get-tuple-element.17) | copy-start | bytes 49156
  348.9 5.7 %copy-start.4 = (bf16[8,4,1,256]{3,2,0,1:T(2,128)(2,1)S(1)}, bf16[8,4,1,256]{3,2,0,1:T(2,128)(2,1)}, u32[]{:S(2)}) copy-start(bf16[8,4,1,256]{3,2,0,1:T(2,128)(2,1)} %get-tuple-element.18) | copy-start | bytes 49156
Sparse Core Ops, SparseCore 0:
  320.1 15.5 reduce-scatter.2
  352.8 20.7 reduce-scatter.4
where the time goes:
time: 384 us; the launch traced here: 382 us
  blocking collectives  284 us (74%)
  waiting for transfers between devices  34 us (9%)
  local copies, waits for them, and re-layouts  26 us (7%)
  between operations  14.3 us (4%)
  matrix products  13.4 us (3%)
  other arithmetic  6.54 us (2%)
  starting transfers between devices  4.3 us (1%)
    pmax x1, blocking collectives, merge_long(): top = lax.pmax(peak, 'seq')  125 us
    psum x1, blocking collectives, merge_long(): lax.psum((total * scale, output * scale[..., None]), 'seq')  124 us
    reduce_scatter x1, waiting for transfers between devices, shards(): lax.psum_scatter(jnp.dot(hidden, w_down, preferred_element_type=jnp.float...  18.3 us
    unnamed x32, local copies, waits for them, and re-layouts  16.5 us
    reduce_scatter x1, waiting for transfers between devices, shards(): lax.psum_scatter(jnp.dot(spread, w_out, preferred_element_type=jnp.float3...  15.6 us
    all_gather x1, blocking collectives, shards(): lax.all_gather(normed, 'req', axis=0, tiled=True)  13.3 us
    all_gather x1, blocking collectives, shards(): lax.all_gather(normed_ffn, 'req', axis=0, tiled=True)  12 us
    all_to_all x1, blocking collectives, shards(): lax.all_to_all(attended, 'req', split_axis=1, concat_axis=0, tiled=True)  9.76 us
  transfers between devices with their start and end apart: 3, of which 2 were waited for; matrix products, arithmetic and copies ran while one was open for 5% of the time, Pallas kernels for 0%

commit v1 on v0

--- a/solution.py
+++ b/solution.py
@@ -112,7 +112,10 @@
     peak, total, output = join(cache_part, fresh)
     attended = output / total[..., None]
     attended = attended.transpose(0, 2, 1, 3).reshape(rows_count, width).astype(jnp.bfloat16)
-    spread = lax.all_to_all(attended, "req", split_axis=1, concat_axis=0, tiled=True)
+    spread = jnp.concatenate(
+        lax.all_to_all(jnp.stack(jnp.split(attended, lax.axis_size("req"), axis=1)), "req", 0, 0),
+        axis=0,
+    )
     mixed = rows + lax.psum_scatter(
         jnp.dot(spread, w_out, preferred_element_type=jnp.float32),
         "req",

time: 384 us -> 384 us (level)
  no operation moved by 1% of the time
where the time goes in v1:
time: 384 us; the launch traced here: 382 us
  blocking collectives  284 us (74%)
  waiting for transfers between devices  34 us (9%)
  local copies, waits for them, and re-layouts  26 us (7%)
  between operations  14.3 us (4%)
  matrix products  13.4 us (3%)
  other arithmetic  6.55 us (2%)
  starting transfers between devices  4.3 us (1%)
    pmax x1, blocking collectives, merge_long(): top = lax.pmax(peak, 'seq')  125 us
    psum x1, blocking collectives, merge_long(): lax.psum((total * scale, output * scale[..., None]), 'seq')  124 us
    reduce_scatter x1, waiting for transfers between devices, shards(): lax.psum_scatter(jnp.dot(hidden, w_down, preferred_element_type=jnp.float...  18.3 us
    unnamed x32, local copies, waits for them, and re-layouts  16.5 us
    reduce_scatter x1, waiting for transfers between devices, shards(): lax.psum_scatter(jnp.dot(spread, w_out, preferred_element_type=jnp.float3...  15.6 us
    all_gather x1, blocking collectives, shards(): lax.all_gather(normed, 'req', axis=0, tiled=True)  13.3 us
    all_gather x1, blocking collectives, shards(): lax.all_gather(normed_ffn, 'req', axis=0, tiled=True)  12 us
    all_to_all x1, blocking collectives, shards(): lax.all_to_all(jnp.stack(jnp.split(attended, lax.axis_size('req'), axis=1...  9.76 us
  transfers between devices with their start and end apart: 3, of which 2 were waited for; matrix products, arithmetic and copies ran while one was open for 5% of the time, Pallas kernels for 0%

profile of v1, /device:TPU:0, one launch (start us, length us, event | category | flops | bytes accessed | tf_op | source)
XLA Modules:
  0.0 382.5 jit_solution(9804030382740199844)
XLA Ops:
  7.2 0.0 copy-start
  7.2 0.0 copy-start.11
  7.2 1.0 fusion.115
  8.2 0.1 div.23
  8.3 0.9 multiply_reduce_fusion.1
  9.2 0.8 maximum_convert_fusion
  10.0 0.1 rsqrt.20
  10.1 0.8 multiply_convert_fusion.1
  10.8 13.3 %all_gather.6 = bf16[64,1024]{1,0:T(8,128)(2,1)S(1)} all-gather(bf16[16,1024]{1,0:T(8,128)(2,1)S(1)} %multiply_convert_fusion.1), channel_id=1, replica_groups=mesh['req'=4,'seq'=32] {'req'}, dimensions={0}, use_global_device_ids=true | all-gather | bytes 163840 | tf_op jit(solution)/shard_map/all_gather | solution.py:93
  24.2 2.4 fusion.7
  26.5 4.3 %all-to-all-start = ((bf16[4,16,768]{2,1,0:T(8,128)(2,1)}), bf16[4,16,768]{2,1,0:T(8,128)(2,1)S(1)}, u32[]{:S(2)}, u32[]{:S(2)}) async-start(bf16[4,16,768]{2,1,0:T(8,128)(2,1)} %bitcast), calls=%async_computation | async-start | bytes 196608 | tf_op jit(solution)/shard_map/all_to_all | solution.py:97
  30.8 0.1 iota_compare_fusion
  30.9 1.5 copy.146
  32.4 2.3 copy.148
  34.7 6.2 %copy.142 = bf16[2,1024,1024]{1,2,0:T(8,128)(2,1)} copy(bf16[2,1024,1024]{2,1,0:T(8,128)(2,1)} %param.18) | data formatting | bytes 8388608 | tf_op args[2]
  40.9 6.2 %copy.144 = bf16[2,1024,1024]{1,2,0:T(8,128)(2,1)} copy(bf16[2,1024,1024]{2,1,0:T(8,128)(2,1)} %param.19) | data formatting | bytes 8388608 | tf_op args[3]
  47.1 0.0 copy-done.12
  47.1 0.1 broadcast_compare_fusion
  47.2 0.0 all-to-all-done
  47.3 0.8 fusion.120
  48.1 0.1 fusion.121
  48.3 0.1 reshape_reshape_squeeze.6
  48.4 0.7 reshape_squeeze.2
  49.2 1.0 fusion.68
  50.2 0.2 copy.153
  50.4 0.1 fusion.79
  50.5 0.1 fusion.80
  50.6 0.1 copy.165
  50.7 0.8 copy.145
  51.5 0.1 slice.66
  51.6 0.8 copy.141
  52.4 0.1 slice.64
  52.5 0.7 reshape_reshape_squeeze.7
  53.2 0.1 copy.166
  53.3 0.8 copy.157
  54.1 0.3 fusion.123
  54.5 125.1 %pmax.7 = f32[2,16,4]{2,1,0:T(8,128)S(1)} all-reduce(f32[2,16,4]{2,1,0:T(8,128)S(1)} %get-tuple-element.32), channel_id=1, replica_groups=mesh['req'=4,'seq'=32] {'seq'}, use_global_device_ids=true, to_apply=%region_4.5 | all-reduce | flops 128 | bytes 1024 | tf_op jit(solution)/shard_map/pmax | solution.py:41
  179.5 0.2 fusion.64
  179.7 3.1 fusion.124
  182.8 0.4 fusion.15
  183.2 1.2 fusion.17
  184.5 0.4 convolution_multiply_fusion.3
  184.9 123.9 %all-reduce = (f32[2,16,4,64]{3,2,1,0:T(4,128)S(1)}, f32[2,16,4]{2,1,0:T(8,128)S(1)}) all-reduce(f32[2,16,4,64]{3,2,1,0:T(4,128)S(1)} %convolution_multiply_fusion.3, f32[2,16,4]{2,1,0:T(8,128)S(1)} %get-tuple-element.13), channel_id=1, replica_groups=mesh['req'=4,'seq'=32] {'seq'}, use_global_device_ids=true, to_apply=%region_5.6 | all-reduce | flops 8320 | bytes 66560 | tf_op jit(solution)/shard_map/psum | solution.py:43
  308.8 0.3 fusion.14
  309.1 0.1 convert_element_type.53
  309.3 9.8 %all_to_all.21 = bf16[4,16,256]{2,1,0:T(8,128)(2,1)S(1)} all-to-all(bf16[4,16,256]{2,1,0:T(8,128)(2,1)S(1)} %pad_maximum_fusion.1), channel_id=1, replica_groups=mesh['req'=4,'seq'=32] {'req'}, dimensions={0} | all-to-all | bytes 65536 | tf_op jit(solution)/shard_map/all_to_all | solution.py:116
  319.0 0.9 fusion.127
  319.9 0.0 reduce-scatter.3.cloned.1.call-update
  320.0 0.0 reduce-scatter.5.cloned.1.call-start
  320.0 15.6 %reduce-scatter.3.cloned.1.call-done = f32[16,1024]{1,0:T(8,128)} async-done(((f32[64,1024]{1,0:T(8,128)}), f32[16,1024]{1,0:T(8,128)}) %reduce-scatter.3.cloned.1.call-update) | async-done | bytes 65552 | tf_op jit(solution)/shard_map/reduce_scatter | solution.py:119
  335.7 1.0 fusion.116
  336.6 0.2 multiply_reduce_fusion
  336.8 0.1 multiply_convert_fusion
  336.9 12.0 %all_gather.7 = bf16[64,1024]{1,0:T(8,128)(2,1)S(1)} all-gather(bf16[16,1024]{1,0:T(8,128)(2,1)S(1)} %multiply_convert_fusion), channel_id=1, replica_groups=mesh['req'=4,'seq'=32] {'req'}, dimensions={0}, use_global_device_ids=true | all-gather | bytes 163840 | tf_op jit(solution)/shard_map/all_gather | solution.py:128
  348.9 3.7 fusion.32
  352.6 0.0 reduce-scatter.5.cloned.1.call-update
  352.7 0.6 slice.81
  353.3 0.6 slice.79
  354.0 0.6 slice.77
  354.6 0.6 slice.75
  355.2 18.3 %reduce-scatter.5.cloned.1.call-done = f32[16,1024]{1,0:T(8,128)} async-done(((f32[64,1024]{1,0:T(8,128)}), f32[16,1024]{1,0:T(8,128)}) %reduce-scatter.5.cloned.1.call-update) | async-done | bytes 65552 | tf_op jit(solution)/shard_map/reduce_scatter | solution.py:134
  373.6 0.8 add_convert_fusion
  374.4 0.6 slice.73
  375.0 0.6 slice.71
  (45 shorter events, 0.4 us)
Async XLA Ops:
  7.2 341.7 %copy-start = (bf16[1024,1024]{1,0:T(8,128)(2,1)S(1)}, bf16[1024,1024]{1,0:T(8,128)(2,1)}, u32[]{:S(2)}) copy-start(bf16[1024,1024]{1,0:T(8,128)(2,1)} %param.31) | copy-start | bytes 6291460
  7.2 23.6 %copy-start.11 = (s32[2]{0:T(128)S(1)}, s32[2]{0:T(128)}, u32[]{:S(2)}) copy-start(s32[2]{0:T(128)} %param.22) | copy-start | bytes 28
  26.5 20.7 %all-to-all-start = ((bf16[4,16,768]{2,1,0:T(8,128)(2,1)}), bf16[4,16,768]{2,1,0:T(8,128)(2,1)S(1)}, u32[]{:S(2)}, u32[]{:S(2)}) async-start(bf16[4,16,768]{2,1,0:T(8,128)(2,1)} %bitcast), calls=%async_computation | async-start | bytes 196608 | tf_op jit(solution)/shard_map/all_to_all | solution.py:97
  30.8 304.9 %reduce-scatter.3.cloned.1.call-start = ((), (), s32[]{:S(2)}) async-start(), calls=%async_computation.4 | async-start | bytes 327680 | tf_op jit(solution)/shard_map/reduce_scatter | solution.py:119
  40.9 6.2 %copy-start.12 = (s32[2]{0:T(128)S(1)}, s32[2]{0:T(128)}, u32[]{:S(2)}) copy-start(s32[2]{0:T(128)} %param.23) | copy-start | bytes 28
  179.5 3.7 copy-start.1
  182.8 1.7 copy-start.2
  183.2 125.6 %copy-start.8 = (bf16[4,16,4,4]{3,2,1,0:T(4,128)(2,1)S(1)}, bf16[4,16,4,4]{3,2,1,0:T(4,128)(2,1)}, u32[]{:S(2)}) copy-start(bf16[4,16,4,4]{3,2,1,0:T(4,128)(2,1)} %copy.157) | copy-start | bytes 6148
  183.2 125.6 %copy-start.9 = (bf16[4,4,16,64]{3,2,1,0:T(8,128)(2,1)S(1)}, bf16[4,4,16,64]{3,2,1,0:T(8,128)(2,1)}, u32[]{:S(2)}) copy-start(bf16[4,4,16,64]{3,2,1,0:T(8,128)(2,1)} %reshape_reshape_squeeze.7) | copy-start | bytes 98308
  184.4 134.6 %copy-start.3 = (bf16[256,1024]{1,0:T(8,128)(2,1)S(1)}, bf16[256,1024]{1,0:T(8,128)(2,1)}, u32[]{:S(2)}) copy-start(bf16[256,1024]{1,0:T(8,128)(2,1)} %param.29) | copy-start | bytes 1572868
  184.4 152.4 %copy-start.10 = (f32[1024]{0:T(1024)S(1)}, f32[1024]{0:T(1024)}, u32[]{:S(2)}) copy-start(f32[1024]{0:T(1024)} %param.25) | copy-start | bytes 12292
  320.0 53.6 %reduce-scatter.5.cloned.1.call-start = ((), (), s32[]{:S(2)}) async-start(), calls=%async_computation.5 | async-start | bytes 327680 | tf_op jit(solution)/shard_map/reduce_scatter | solution.py:134
  348.9 3.8 copy-start.7
  348.9 4.4 %copy-start.6 = (bf16[8,4,1,256]{3,2,0,1:T(2,128)(2,1)S(1)}, bf16[8,4,1,256]{3,2,0,1:T(2,128)(2,1)}, u32[]{:S(2)}) copy-start(bf16[8,4,1,256]{3,2,0,1:T(2,128)(2,1)} %get-tuple-element.16) | copy-start | bytes 49156
  348.9 5.0 %copy-start.5 = (bf16[8,4,1,256]{3,2,0,1:T(2,128)(2,1)S(1)}, bf16[8,4,1,256]{3,2,0,1:T(2,128)(2,1)}, u32[]{:S(2)}) copy-start(bf16[8,4,1,256]{3,2,0,1:T(2,128)(2,1)} %get-tuple-element.17) | copy-start | bytes 49156
  348.9 5.7 %copy-start.4 = (bf16[8,4,1,256]{3,2,0,1:T(2,128)(2,1)S(1)}, bf16[8,4,1,256]{3,2,0,1:T(2,128)(2,1)}, u32[]{:S(2)}) copy-start(bf16[8,4,1,256]{3,2,0,1:T(2,128)(2,1)} %get-tuple-element.18) | copy-start | bytes 49156
Sparse Core Ops, SparseCore 0:
  320.1 15.5 reduce-scatter.2
  352.8 20.7 reduce-scatter.4
